TPU v7x, 512 devices: a whole 4x4x16 slice. The times are simulated.
512 devices in a mesh: req: 8 (over z_lo), row: 8 (over x, core), col: 8 (over y, z_hi).
Axes of the slice: x: 4, y: 4, z: 16 (z_hi: 2, z_lo: 8; z = z_hi * 8 + z_lo), core: 2. Of those that a mesh axis runs over, the one named last changes fastest.
Arguments:
- tokens: bfloat16 [1792, 32768], P('col', ('req', 'row')), may hold values from -6 to 6
- qkv_weight: bfloat16 [1792, 2304], P('col', 'row'), may hold values from -0.125 to 0.125
- out_weight: bfloat16 [1792, 1792], P('row', 'col'), may hold values from -0.125 to 0.125
- head_gain: float32 [1792], P('row'), may hold values from 0.1 to 1.9
- prefix_keys: bfloat16 [24, 256, 8192], P('req', 'row', 'col'), may hold values from -6 to 6
- prefix_values: bfloat16 [24, 1792, 8192], P('req', 'row', 'col'), may hold values from -6 to 6
- suffix_len: int32 [64], P(('req', 'col')), may hold values from 1 to 512, 24576 in all
- prefix_owner: int32 [64], P(('req', 'col')), may hold values from 0 to 23
Outputs:
- layer_out: bfloat16 [1792, 32768], P('col', ('req', 'row'))
Inputs may be any that keep to these rules, and one draw needn't show every extreme that they name: `suffix_len`: the longest suffix has exactly 512 live tokens.
All inputs are finite; a program needn't handle non-finite values. No bound on the sum of `suffix_len` on one device may be relied on, other than what follows from the above.
Results may differ from a plain program's by a relative error of at most 0.015.
Values may be sent and summed in bfloat16 or wider, within the bound.
No kernel may reach another device: no remote copies, remote signals or barrier semaphores. Data moves between devices by JAX's collectives and lax.ppermute only.
A program may use at most 64 MiB of HBM per device.

v0:
```python
import jax
import jax.numpy as jnp
from jax import lax
from jax.sharding import PartitionSpec as P

FEAT = 16
SLOTS = 512
HD = 112
epsilon = 1e-05


def feature_map(values_in):
    feature_count = values_in.shape[-1]
    squares = (values_in[..., :, None] * values_in[..., None, :]).reshape(
        values_in.shape[:-1] + (feature_count * feature_count,)
    )
    constant = jnp.ones(values_in.shape[:-1] + (1,), jnp.float32)
    linear = values_in * feature_count ** (-0.25)
    quadratic = squares * (0.5**0.5 / feature_count**0.5)
    return jnp.concatenate([constant, linear, quadratic], axis=-1).astype(jnp.bfloat16)


def feature_columns(values_in):
    feature_count = values_in.shape[-2]
    length = values_in.shape[-1]
    squares = (values_in[..., :, None, :] * values_in[..., None, :, :]).reshape(
        values_in.shape[:-2] + (feature_count * feature_count, length)
    )
    constant = jnp.ones(values_in.shape[:-2] + (1, length), jnp.float32)
    linear = values_in * feature_count ** (-0.25)
    quadratic = squares * (0.5**0.5 / feature_count**0.5)
    return jnp.concatenate([constant, linear, quadratic], axis=-2).astype(jnp.bfloat16)


def shards(
    tokens, qkv_weight, out_weight, head_gain, prefix_keys, prefix_values, suffix_len, prefix_owner
):
    heads_here = head_gain.shape[0] // HD
    partial_proj = lax.dot_general(
        lax.all_gather(tokens, "row", axis=1, tiled=True),
        qkv_weight,
        (((0,), (0,)), ((), ())),
        preferred_element_type=jnp.float32,
    )
    projected = lax.psum_scatter(
        partial_proj.astype(jnp.bfloat16), "col", scatter_dimension=0, tiled=True
    )
    requests = projected.shape[0] // SLOTS
    projected = projected.reshape(requests, SLOTS, heads_here, 2 * FEAT + HD)
    queries = projected[..., :FEAT]
    keys_now = projected[..., FEAT : 2 * FEAT]
    values_now = projected[..., 2 * FEAT :]
    pref_here = prefix_keys.shape[0]
    plen_here = prefix_keys.shape[2]
    feats_cached = feature_columns(
        prefix_keys.reshape(pref_here, heads_here, FEAT, plen_here).astype(jnp.float32)
    )
    values_cached = prefix_values.reshape(pref_here, heads_here, HD, plen_here)
    partial_state = jnp.einsum(
        "phet,phvt->phev", feats_cached, values_cached, preferred_element_type=jnp.float32
    )
    summed_state = lax.psum(partial_state.astype(jnp.bfloat16), "col").astype(jnp.float32)
    states = lax.all_gather(summed_state.astype(jnp.bfloat16), "req", axis=0, tiled=True).astype(
        summed_state.dtype
    )
    prefixes = states.shape[0]
    selector = (prefix_owner[:, None] == jnp.arange(prefixes, dtype=jnp.int32)[None, :]).astype(
        jnp.float32
    )
    chosen = jnp.einsum("rp,phev->rhev", selector, states, precision=lax.Precision.HIGHEST)
    feats_query = feature_map(queries.astype(jnp.float32)).astype(jnp.float32)
    carried = jnp.einsum("rthe,rhev->rthv", feats_query, chosen, precision=lax.Precision.HIGHEST)
    scores = jnp.einsum("rthf,rshf->rhts", queries, keys_now, preferred_element_type=jnp.float32)
    weights = 1.0 + scores * FEAT ** (-0.5) + scores * scores * (0.5 / FEAT)
    positions = jnp.arange(SLOTS, dtype=jnp.int32)
    allowed = (positions[None, None, :] <= positions[None, :, None]) & (
        positions[None, None, :] < suffix_len[:, None, None]
    )
    weights = jnp.where(allowed[:, None], weights, 0.0).astype(jnp.bfloat16)
    within = jnp.einsum("rhts,rshv->rthv", weights, values_now, preferred_element_type=jnp.float32)
    active = (positions[None, :] < suffix_len[:, None])[:, :, None, None]
    attended = jnp.where(active, carried + within, 0.0)
    inverse_rms = lax.rsqrt(jnp.mean(attended * attended, axis=-1, keepdims=True) + epsilon)
    gains = head_gain.reshape(heads_here, HD)
    normed = (
        (attended * inverse_rms * gains)
        .astype(jnp.bfloat16)
        .reshape(requests * SLOTS, heads_here * HD)
    )
    out_terms = lax.dot_general(
        out_weight,
        lax.all_gather(normed, "col", axis=0, tiled=True),
        (((0,), (1,)), ((), ())),
        preferred_element_type=jnp.float32,
    )
    mixed_sums = lax.psum_scatter(
        out_terms.astype(jnp.bfloat16), "row", scatter_dimension=1, tiled=True
    ).astype(jnp.float32)
    return (tokens.astype(jnp.float32) + mixed_sums).astype(jnp.bfloat16)


def solution(mesh):
    in_specs = (
        P("col", ("req", "row")),
        P("col", "row"),
        P("row", "col"),
        P("row"),
        P("req", "row", "col"),
        P("req", "row", "col"),
        P(("req", "col")),
        P(("req", "col")),
    )
    out_specs = P("col", ("req", "row"))
    return jax.shard_map(shards, mesh=mesh, in_specs=in_specs, out_specs=out_specs, check_vma=False)
```

profile of v0, /device:TPU:8, one launch (start us, length us, event | category | flops | bytes accessed | tf_op | source)
XLA Modules:
  0.0 532.3 jit_solution(16961379070519875924)
XLA Ops:
  7.4 1.1 convert.24
  8.4 1.0 multiply_convert_fusion.3
  9.4 0.9 multiply_convert_fusion
  10.3 1.3 fusion.1
  11.7 1.1 copy.20
  12.8 0.5 all-gather.6.cloned.1.call-update
  13.4 182.7 %all-reduce.2.cloned.1.call-done = bf16[3,2,273,112]{3,1,2,0:T(2,128)(2,1)} async-done(((bf16[3,2,273,112]{3,1,2,0:T(2,128)(2,1)}), bf16[3,2,273,112]{3,1,2,0:T(2,128)(2,1)}) %all-reduce.2.cloned.1.call-update) | async-done | bytes 366928 | tf_op jit(solution)/shard_map/psum | solution.py:62
  196.2 3.7 convolution_convert_fusion
  201.2 0.1 mul.133
  201.3 0.1 fusion.17
  201.4 129.0 %all-gather.4.cloned.1.call-done = bf16[24,2,273,112]{3,1,2,0:T(2,128)(2,1)} async-done(((bf16[3,2,273,112]{3,1,2,0:T(2,128)(2,1)}), bf16[24,2,273,112]{3,1,2,0:T(2,128)(2,1)}) %all-gather.4.cloned.1.call-update) | async-done | bytes 2935312 | tf_op jit(solution)/shard_map/all_gather | solution.py:63
  330.4 2.7 fusion.6
  333.2 46.1 %reduce-scatter.3.cloned.1.call-done = bf16[512,288]{0,1:T(8,128)(2,1)} async-done(((bf16[4096,288]{0,1:T(8,128)(2,1)}), bf16[512,288]{0,1:T(8,128)(2,1)}) %reduce-scatter.3.cloned.1.call-update) | async-done | bytes 294928 | tf_op jit(solution)/shard_map/reduce_scatter | solution.py:45
  379.3 0.8 convert_bitcast_fusion
  380.0 0.8 fusion.27
  380.8 1.9 fusion.9
  382.7 0.1 multiply_convert_fusion.1
  382.9 0.8 multiply_reduce_fusion
  383.7 0.8 multiply_convert_fusion.2
  384.5 0.0 reduce-scatter.5.cloned.1.call-start
  384.6 99.5 %all-gather.8.cloned.1.call-done = bf16[4096,224]{0,1:T(8,128)(2,1)} async-done(((bf16[512,224]{0,1:T(8,128)(2,1)}), bf16[4096,224]{0,1:T(8,128)(2,1)}) %all-gather.8.cloned.1.call-update) | async-done | bytes 1835024 | tf_op jit(solution)/shard_map/all_gather | solution.py:92
  484.1 3.4 fusion
  487.6 35.6 %reduce-scatter.5.cloned.1.call-done = bf16[224,512]{1,0:T(8,128)(2,1)} async-done(((bf16[224,4096]{1,0:T(8,128)(2,1)}), bf16[224,512]{1,0:T(8,128)(2,1)}) %reduce-scatter.5.cloned.1.call-update) | async-done | bytes 229392 | tf_op jit(solution)/shard_map/reduce_scatter | solution.py:96
  523.2 1.7 add_convert_fusion
  (24 shorter events, 0.3 us)
Async XLA Ops:
  7.4 3.0 copy-start
  7.4 188.7 %all-reduce.2.cloned.1.call-start = ((), (), s32[]{:S(2)}) async-start(), calls=%async_computation.2 | async-start | bytes 838656 | tf_op jit(solution)/shard_map/psum | solution.py:62
  10.3 185.8 %copy-start.2 = (bf16[224,288]{0,1:T(8,128)(2,1)S(1)}, bf16[224,288]{0,1:T(8,128)(2,1)}, u32[]{:S(2)}) copy-start(bf16[224,288]{0,1:T(8,128)(2,1)} %param.9) | copy-start | bytes 387076
  12.8 183.4 %all-gather.6.cloned.1.call-start = ((), (), s32[]{:S(2)}) async-start(), calls=%async_computation.4 | async-start | bytes 2064384 | tf_op jit(solution)/shard_map/all_gather | solution.py:40
  13.3 317.1 %all-gather.4.cloned.1.call-start = ((), (), s32[]{:S(2)}) async-start(), calls=%async_computation.3 | async-start | bytes 3773952 | tf_op jit(solution)/shard_map/all_gather | solution.py:63
  196.1 183.2 %reduce-scatter.3.cloned.1.call-start = ((), (), s32[]{:S(2)}) async-start(), calls=%async_computation.5 | async-start | bytes 2654208 | tf_op jit(solution)/shard_map/reduce_scatter | solution.py:45
  199.9 1.4 copy-start.4
  199.9 284.2 %all-gather.8.cloned.1.call-start = ((), (), s32[]{:S(2)}) async-start(), calls=%async_computation.6 | async-start | bytes 2064384 | tf_op jit(solution)/shard_map/all_gather | solution.py:92
  382.7 101.4 %copy-start.3 = (bf16[224,224]{1,0:T(8,128)(2,1)S(1)}, bf16[224,224]{1,0:T(8,128)(2,1)}, u32[]{:S(2)}) copy-start(bf16[224,224]{1,0:T(8,128)(2,1)} %param.10) | copy-start | bytes 301060
  384.5 138.7 %copy-start.1 = (bf16[224,512]{1,0:T(8,128)(2,1)S(1)}, bf16[224,512]{1,0:T(8,128)(2,1)}, u32[]{:S(2)}) copy-start(bf16[224,512]{1,0:T(8,128)(2,1)} %param.8) | copy-start | bytes 688132
  384.5 138.7 %reduce-scatter.5.cloned.1.call-start = ((), (), s32[]{:S(2)}) async-start(), calls=%async_computation.7 | async-start | bytes 2064384 | tf_op jit(solution)/shard_map/reduce_scatter | solution.py:96
Sparse Core Ops, SparseCore 0:
  12.9 183.1 all-reduce.1
  201.6 177.6 reduce-scatter.2
  384.6 99.4 all-gather.7
Sparse Core Ops, SparseCore 1:
  15.4 36.7 all-gather.5
  196.1 134.2 all-gather.3
  487.7 35.5 reduce-scatter.4
where the time goes:
time: 533 us; the launch traced here: 532 us
  waiting for transfers between devices  494 us (93%)
  between operations  16.2 us (3%)
  matrix products  13.9 us (3%)
  other arithmetic  7.12 us (1%)
    psum x1, waiting for transfers between devices, shards(): lax.psum(partial_state.astype(jnp.bfloat16), 'col').astype(jnp.float32)  183 us
    all_gather x1, waiting for transfers between devices, shards(): lax.all_gather(summed_state.astype(jnp.bfloat16), 'req', axis=0, tiled=True)  129 us
    all_gather x1, waiting for transfers between devices, shards(): lax.all_gather(normed, 'col', axis=0, tiled=True)  99.5 us
    reduce_scatter x1, waiting for transfers between devices, shards(): lax.psum_scatter(partial_proj.astype(jnp.bfloat16), 'col', scatter_dimens...  46.1 us
    reduce_scatter x1, waiting for transfers between devices, shards(): lax.psum_scatter(out_terms.astype(jnp.bfloat16), 'row', scatter_dimension...  35.6 us
  transfers between devices with their start and end apart: 6, of which 5 were waited for; matrix products, arithmetic and copies ran while one was open for 1% of the time, Pallas kernels for 0%

commit v1 on v0

--- a/solution.py
+++ b/solution.py
@@ -59,7 +59,9 @@
     partial_state = jnp.einsum(
         "phet,phvt->phev", feats_cached, values_cached, preferred_element_type=jnp.float32
     )
-    summed_state = lax.psum(partial_state.astype(jnp.bfloat16), "col").astype(jnp.float32)
+    summed_state = jnp.sum(
+        lax.all_gather(partial_state.astype(jnp.bfloat16), "col"), axis=0
+    ).astype(jnp.float32)
     states = lax.all_gather(summed_state.astype(jnp.bfloat16), "req", axis=0, tiled=True).astype(
         summed_state.dtype
     )

time: 533 us -> 597 us (1.12)
  waiting for transfers between devices: 494 us -> 553 us
  other arithmetic: 7.12 us -> 13.9 us
    psum x1 -> x0, waiting for transfers between devices: 183 us -> none  [shards(): lax.psum(partial_state.astype(jnp.bfloat16), 'col').astype(jnp.float32)]
    all_gather x0 -> x1, waiting for transfers between devices: none -> 152 us  [shards(): lax.all_gather(partial_state.astype(jnp.bfloat16), 'col')]
    reduce_scatter x1, waiting for transfers between devices: 46.1 us -> 150 us  [shards(): lax.psum_scatter(partial_proj.astype(jnp.bfloat16), 'col', scatter_dimens...]
    all_gather x1, waiting for transfers between devices: 129 us -> 77.3 us  [shards(): lax.all_gather(summed_state.astype(jnp.bfloat16), 'req', axis=0, tiled=True)]
    all_gather x1, waiting for transfers between devices: 0.03 us -> 33.8 us  [shards(): lax.all_gather(tokens, 'row', axis=1, tiled=True)]
    reduce_sum x0 -> x1, other arithmetic: none -> 6.87 us  [shards(): jnp.sum(lax.all_gather(partial_state.astype(jnp.bfloat16), 'col'), axis=0)]
  transfers between devices with their start and end apart: 6 -> 6, of which waited for: 5 -> 6; matrix products, arithmetic and copies ran while one was open for 1% -> 3% of each run, Pallas kernels for 0% -> 0%
where the time goes in v1:
time: 597 us
  waiting for transfers between devices  553 us (93%)
  between operations  14.9 us (2%)
  other arithmetic  13.9 us (2%)
  matrix products  13.9 us (2%)
    all_gather x1, waiting for transfers between devices, shards(): lax.all_gather(partial_state.astype(jnp.bfloat16), 'col')  152 us
    reduce_scatter x1, waiting for transfers between devices, shards(): lax.psum_scatter(partial_proj.astype(jnp.bfloat16), 'col', scatter_dimens...  150 us
    all_gather x1, waiting for transfers between devices, shards(): lax.all_gather(normed, 'col', axis=0, tiled=True)  103 us
    all_gather x1, waiting for transfers between devices, shards(): lax.all_gather(summed_state.astype(jnp.bfloat16), 'req', axis=0, tiled=True)  77.3 us
    reduce_scatter x1, waiting for transfers between devices, shards(): lax.psum_scatter(out_terms.astype(jnp.bfloat16), 'row', scatter_dimension...  35.8 us
    all_gather x1, waiting for transfers between devices, shards(): lax.all_gather(tokens, 'row', axis=1, tiled=True)  33.8 us
  transfers between devices with their start and end apart: 6, of which 6 were waited for; matrix products, arithmetic and copies ran while one was open for 3% of the time, Pallas kernels for 0%

profile of v1, /device:TPU:8, one launch (start us, length us, event | category | flops | bytes accessed | tf_op | source)
XLA Modules:
  0.0 596.8 jit_solution(17926042103733562626)
XLA Ops:
  6.5 0.7 all-gather.8.cloned.1.call-update
  7.3 1.0 convert.25
  8.3 1.0 multiply_convert_fusion.3
  9.2 0.9 multiply_convert_fusion
  10.2 1.3 fusion.10
  11.5 1.1 copy.9
  12.6 33.8 %all-gather.8.cloned.1.call-done = bf16[224,4096]{1,0:T(8,128)(2,1)} async-done(((bf16[224,512]{1,0:T(8,128)(2,1)}), bf16[224,4096]{1,0:T(8,128)(2,1)}) %all-gather.8.cloned.1.call-update) | async-done | bytes 1835024 | tf_op jit(solution)/shard_map/all_gather | solution.py:40
  46.4 3.7 convolution_convert_fusion
  50.2 152.4 %all-gather.12.cloned.1.call-done = bf16[24,2,273,112]{3,1,2,0:T(2,128)(2,1)} async-done(((bf16[3,2,273,112]{3,1,2,0:T(2,128)(2,1)}), bf16[24,2,273,112]{3,1,2,0:T(2,128)(2,1)}) %all-gather.12.cloned.1.call-update) | async-done | bytes 2935312 | tf_op jit(solution)/shard_map/all_gather | solution.py:63
  202.5 6.9 %reduce_sum.21 = bf16[3,2,273,112]{3,1,2,0:T(2,128)(2,1)} reduce(bf16[8,3,2,273,112]{4,2,3,1,0:T(2,128)(2,1)} %bitcast.55, bf16[]{:T(256)} %constant.4.clone.1), dimensions={0}, to_apply=%region_0.0 | reduce | flops 1284192 | bytes 3302210 | tf_op jit(solution)/shard_map/reduce_sum | solution.py:62
  210.8 0.1 mul.133
  210.9 149.8 %reduce-scatter.3.cloned.1.call-done = bf16[512,288]{0,1:T(8,128)(2,1)} async-done(((bf16[4096,288]{0,1:T(8,128)(2,1)}), bf16[512,288]{0,1:T(8,128)(2,1)}) %reduce-scatter.3.cloned.1.call-update) | async-done | bytes 294928 | tf_op jit(solution)/shard_map/reduce_scatter | solution.py:45
  360.7 0.8 fusion.30
  361.5 0.8 convert_bitcast_fusion
  362.3 0.1 multiply_convert_fusion.1
  362.4 1.9 fusion.9
  364.3 77.3 %all-gather.6.cloned.1.call-done = bf16[24,2,273,112]{3,1,2,0:T(2,128)(2,1)} async-done(((bf16[3,2,273,112]{3,1,2,0:T(2,128)(2,1)}), bf16[24,2,273,112]{3,1,2,0:T(2,128)(2,1)}) %all-gather.6.cloned.1.call-update) | async-done | bytes 2935312 | tf_op jit(solution)/shard_map/all_gather | solution.py:65
  441.6 2.7 fusion.6
  444.3 0.8 multiply_reduce_fusion
  445.2 0.8 multiply_convert_fusion.2
  446.1 103.0 %all-gather.10.cloned.1.call-done = bf16[4096,224]{0,1:T(8,128)(2,1)} async-done(((bf16[512,224]{0,1:T(8,128)(2,1)}), bf16[4096,224]{0,1:T(8,128)(2,1)}) %all-gather.10.cloned.1.call-update) | async-done | bytes 1835024 | tf_op jit(solution)/shard_map/all_gather | solution.py:94
  549.1 3.4 fusion
  552.5 35.8 %reduce-scatter.5.cloned.1.call-done = bf16[224,512]{1,0:T(8,128)(2,1)} async-done(((bf16[224,4096]{1,0:T(8,128)(2,1)}), bf16[224,512]{1,0:T(8,128)(2,1)}) %reduce-scatter.5.cloned.1.call-update) | async-done | bytes 229392 | tf_op jit(solution)/shard_map/reduce_scatter | solution.py:98
  588.3 1.7 add_convert_fusion
  (25 shorter events, 0.4 us)
Async XLA Ops:
  6.5 3.6 copy-start
  6.5 39.9 %all-gather.8.cloned.1.call-start = ((), (), s32[]{:S(2)}) async-start(), calls=%async_computation.3 | async-start | bytes 2064384 | tf_op jit(solution)/shard_map/all_gather | solution.py:40
  7.3 195.3 %all-gather.12.cloned.1.call-start = ((), (), s32[]{:S(2)}) async-start(), calls=%async_computation.7 | async-start | bytes 3773952 | tf_op jit(solution)/shard_map/all_gather | solution.py:63
  10.2 36.2 %copy-start.2 = (bf16[224,288]{0,1:T(8,128)(2,1)S(1)}, bf16[224,288]{0,1:T(8,128)(2,1)}, u32[]{:S(2)}) copy-start(bf16[224,288]{0,1:T(8,128)(2,1)} %param.9) | copy-start | bytes 387076
  12.6 348.2 %reduce-scatter.3.cloned.1.call-start = ((), (), s32[]{:S(2)}) async-start(), calls=%async_computation.4 | async-start | bytes 2654208 | tf_op jit(solution)/shard_map/reduce_scatter | solution.py:45
  50.1 391.5 %all-gather.6.cloned.1.call-start = ((), (), s32[]{:S(2)}) async-start(), calls=%async_computation.2 | async-start | bytes 3773952 | tf_op jit(solution)/shard_map/all_gather | solution.py:65
  202.5 8.2 %copy-start.4 = (f32[224]{0:T(256)S(1)}, f32[224]{0:T(256)}, u32[]{:S(2)}) copy-start(f32[224]{0:T(256)} %param.11) | copy-start | bytes 2692
  209.4 339.6 %all-gather.10.cloned.1.call-start = ((), (), s32[]{:S(2)}) async-start(), calls=%async_computation.5 | async-start | bytes 2064384 | tf_op jit(solution)/shard_map/all_gather | solution.py:94
  444.3 104.7 %copy-start.3 = (bf16[224,224]{1,0:T(8,128)(2,1)S(1)}, bf16[224,224]{1,0:T(8,128)(2,1)}, u32[]{:S(2)}) copy-start(bf16[224,224]{1,0:T(8,128)(2,1)} %param.10) | copy-start | bytes 301060
  446.0 142.3 %copy-start.1 = (bf16[224,512]{1,0:T(8,128)(2,1)S(1)}, bf16[224,512]{1,0:T(8,128)(2,1)}, u32[]{:S(2)}) copy-start(bf16[224,512]{1,0:T(8,128)(2,1)} %param.8) | copy-start | bytes 688132
  446.0 142.3 %reduce-scatter.5.cloned.1.call-start = ((), (), s32[]{:S(2)}) async-start(), calls=%async_computation.6 | async-start | bytes 2064384 | tf_op jit(solution)/shard_map/reduce_scatter | solution.py:98
Sparse Core Ops, SparseCore 0:
  9.5 36.8 all-gather.7
  49.6 152.8 all-gather.11
  207.2 153.4 reduce-scatter.2
  362.7 78.8 all-gather.5
  446.1 102.8 all-gather.9
  552.6 35.5 reduce-scatter.4
